TPU v7x, 32 devices: a whole 2x2x4 slice. The times are simulated.
32 devices in a mesh: groups: 2 (over x), blk: 16 (over z, y, core).
Axes of the slice: x: 2, y: 2, z: 4, core: 2. Of those that a mesh axis runs over, the one named last changes fastest.
Arguments:
- contacts: float32 [512, 6144], P(('groups', 'blk')), parts along dimension 0, may hold values from 0.1 to 10
- widths: int32 [12288], P('groups'), parts along dimension 0, may hold values from 0 to 3
- masked_bins: int32 [768], P('groups'), parts along dimension 0, may hold values from 0 to 6143, as said below
- row_start: int32 [2], P('groups'), parts along dimension 0, may hold values from 0 to 5888
Outputs:
- correlation: float32 [512, 256], P(('groups', 'blk')), parts along dimension 0
There are 2 independent parts, one for each index of `groups`. A program takes and returns all parts, laid end to end along the dimension named above; each array names one. Nothing has to cross between parts.
Inputs may be any that keep to these rules, and one draw needn't show every extreme that they name: `masked_bins`: distinct bins.
All inputs are finite; a program needn't handle non-finite values.
Results may differ from a plain program's by a relative error of at most 0.00083.
Values may be sent and summed in bfloat16 or wider, within the bound.
No kernel may reach another device: no remote copies, remote signals or barrier semaphores. Data moves between devices by JAX's collectives and lax.ppermute only.
A program may use at most 64 MiB of HBM per device.

v0:
```python
import jax
import jax.numpy as jnp
from jax import lax
from jax.sharding import PartitionSpec as P

WMAX = 3


def with_halo(cells, sides, width):
    for axis, dim in sides:
        count = lax.axis_size(axis)
        ends = count - 1
        head = lax.slice_in_dim(cells, 0, width, axis=dim)
        tail = lax.slice_in_dim(cells, cells.shape[dim] - width, cells.shape[dim], axis=dim)
        cells = jnp.concatenate(
            [
                lax.ppermute(tail, axis, [(i, (i + 1) % count) for i in range(ends)]),
                cells,
                lax.ppermute(head, axis, [((i + 1) % count, i) for i in range(ends)]),
            ],
            axis=dim,
        )
    return cells


def smooth(padded, radius_map):
    rows_here = padded.shape[0] - 2 * WMAX
    col_count = padded.shape[1] - 2 * WMAX
    row_sums = padded[WMAX : WMAX + rows_here]
    smoothed = jnp.zeros((rows_here, col_count), jnp.float32)
    for radius in range(WMAX + 1):
        if radius > 0:
            row_sums = (
                row_sums
                + padded[WMAX - radius : WMAX - radius + rows_here]
                + padded[WMAX + radius : WMAX + radius + rows_here]
            )
        box_sums = row_sums[:, WMAX : WMAX + col_count]
        for offset in range(1, radius + 1):
            box_sums = (
                box_sums
                + row_sums[:, WMAX - offset : WMAX - offset + col_count]
                + row_sums[:, WMAX + offset : WMAX + offset + col_count]
            )
        smoothed = smoothed + jnp.where(
            radius_map == radius, box_sums / float((2 * radius + 1) ** 2), 0.0
        )
    return smoothed


def pair_counts(first_bin, nrows, col_count):
    distance = jnp.arange(col_count, dtype=jnp.int32)
    upper_pairs = jnp.clip(col_count - distance - first_bin, 0, nrows)
    lower_pairs = jnp.clip(first_bin + nrows - distance, 0, nrows)
    pair_total = jnp.where(distance == 0, nrows, upper_pairs + lower_pairs)
    return jnp.maximum(pair_total, 1).astype(jnp.float32)


def mirrored_table(table):
    return jnp.concatenate([table[1:][::-1], table])


def skewed_map(table, window_first, rows_here, col_count):
    span = col_count + rows_here - 1
    window = lax.dynamic_slice_in_dim(mirrored_table(table), window_first, span)
    tiled = jnp.tile(window, rows_here + 1)[: rows_here * (span + 1)]
    shifted = tiled.reshape(rows_here, span + 1)[:, :col_count]
    return shifted[::-1]


def diagonal_totals(smoothed, window_first):
    rows_here = smoothed.shape[0]
    col_count = smoothed.shape[1]
    span = col_count + rows_here - 1
    flipped = jnp.pad(smoothed[::-1], ((0, 0), (0, rows_here)))
    flat = flipped.reshape(rows_here * (col_count + rows_here))[: rows_here * span]
    offsets = jnp.sum(flat.reshape(rows_here, span), axis=0)
    spread = lax.dynamic_update_slice_in_dim(
        jnp.zeros((2 * col_count - 1,), jnp.float32), offsets, window_first, 0
    )
    lower = jnp.concatenate([jnp.zeros((1,), jnp.float32), spread[: col_count - 1][::-1]])
    return spread[col_count - 1 :] + lower


def normalize(smoothed, expected_map, kept_rows, kept_cols):
    ratio = smoothed / expected_map
    kept_total = jnp.sum(kept_cols)
    row_mean = jnp.sum(ratio * kept_cols[None, :], axis=1, keepdims=True) / kept_total
    centred = (ratio - row_mean) * kept_cols[None, :]
    variance = jnp.sum(centred * centred, axis=1, keepdims=True) / kept_total
    zscores = (centred * lax.rsqrt(variance + 1e-05) * kept_rows[:, None]).astype(jnp.bfloat16)
    return (zscores, kept_total)


def cross_block(left, right):
    return lax.dot_general(
        left, right, (((1,), (1,)), ((), ())), preferred_element_type=jnp.float32
    )


def shards(contacts, widths, masked_bins, row_start):
    blocks = lax.axis_size("blk")
    position = lax.axis_index("blk")
    rows_here = contacts.shape[0]
    col_count = contacts.shape[1]
    nbins = rows_here * blocks
    first_row = position * rows_here
    first_bin = row_start[0]
    window_first = col_count - 1 - (first_bin + first_row + rows_here - 1)
    radius_map = skewed_map(widths, window_first, rows_here, col_count)
    padded_rows = with_halo(contacts, (("blk", 0),), WMAX)
    padded = jnp.pad(padded_rows, ((0, 0), (WMAX, WMAX)))
    smoothed = smooth(padded, radius_map)
    local_total = diagonal_totals(smoothed, window_first)
    denominator = pair_counts(first_bin, nbins, col_count)
    expected = lax.psum(local_total, "blk") / denominator
    expected_map = skewed_map(expected, window_first, rows_here, col_count)
    kept_bins = jnp.ones((col_count,), jnp.float32).at[masked_bins].set(0.0)
    kept_rows = lax.dynamic_slice_in_dim(kept_bins, first_bin + first_row, rows_here)
    zscores, kept_total = normalize(smoothed, expected_map, kept_rows, kept_bins)
    return cross_block(zscores, lax.all_gather(zscores, "blk", axis=0, tiled=True)) / kept_total


def solution(mesh):
    return jax.shard_map(
        shards,
        mesh=mesh,
        in_specs=(P(("groups", "blk"), None), P("groups"), P("groups"), P("groups")),
        out_specs=P(("groups", "blk"), None),
        check_vma=False,
    )
```

profile of v0, /device:TPU:0, one launch (start us, length us, event | category | flops | bytes accessed | tf_op | source)
XLA Modules:
  0.0 145.9 jit_solution(1816043342483909816)
XLA Ops:
  6.5 1.1 fusion.14
  7.6 2.4 %collective-permute-start = (f32[3,6144]{1,0:T(4,128)S(1)}, f32[3,6144]{1,0:T(4,128)S(1)}, u32[]{:S(2)}, u32[]{:S(2)}) collective-permute-start(f32[3,6144]{1,0:T(4,128)S(1)} %get-tuple-element.10), channel_id=1, source_target_pairs={{0,1},{1,2},{2,3},{3,4},{4,5},{5,6},{6,7},{7,8},{8,9},{9,10},{10,1... | collective-permute-start | bytes 221192 | tf_op jit(solution)/shard_map/ppermute | solution.py:17
  10.1 1.3 collective-permute-start.1
  12.0 0.7 compare_select_fusion
  12.7 2.9 %scatter_custom_fusion = f32[6144]{0:T(1024)S(1)} fusion(s32[384]{0:T(512)S(1)} %compare_select_fusion, f32[384]{0:T(512)S(1)} %broadcast.30, f32[]{:T(128)} %constant.14.clone.1), kind=kCustom, calls=%fused_computation.47 | custom fusion | bytes 24580 | tf_op jit(solution)/shard_map/scatter | solution.py:118
  15.7 0.7 reduce_sum.38
  16.4 0.8 slice.102
  17.4 0.8 fusion.11
  18.2 0.2 tile.9
  18.5 0.2 reshape.28
  18.8 0.8 rev.19
  19.6 0.3 select_maximum_fusion
  19.9 0.2 slice_add_fusion
  20.2 1.5 %fusion.3 = f32[16,6144]{1,0:T(8,128)S(1)} fusion(f32[16,6150]{1,0:T(8,128)S(1)} %get-tuple-element.7, f32[16,6150]{1,0:T(8,128)S(1)} %get-tuple-element.8, f32[16,6150]{1,0:T(8,128)S(1)} %get-tuple-element.9, f32[16,6144]{1,0:T(8,128)S(1)} %copy-done, s32[16,6144]{1,0:T(8,128)S(1)} %rev.19), kind=kLoop, calls=%fused_computation.16 | loop fusion | flops 2555904 | bytes 7077888 | tf_op jit(solution)/shard_map/add | solution.py:45
  21.7 0.8 rev.20
  22.5 0.3 reshape.29
  22.8 0.3 reshape.30
  23.1 0.5 dynamic_update_slice.3
  23.8 0.1 slice_add_fusion.18
  23.9 63.8 %psum.7 = f32[6144]{0:T(1024)S(1)} all-reduce(f32[6144]{0:T(1024)S(1)} %slice_add_fusion.18), channel_id=1, replica_groups=mesh['groups'=2,'blk'=16] {'blk'}, use_global_device_ids=true, to_apply=%region_1.2 | all-reduce | flops 6144 | bytes 49152 | tf_op jit(solution)/shard_map/psum | solution.py:116
  87.8 0.1 reverse.2
  88.0 0.1 fusion.10
  88.1 0.2 tile.21
  88.4 0.2 reshape.31
  88.7 0.8 rev.23
  89.5 0.2 multiply_reduce_fusion.1
  89.7 0.6 broadcast_divide_fusion
  90.3 0.3 multiply_reduce_fusion
  90.6 0.6 add_rsqrt_fusion
  91.2 0.8 multiply_convert_fusion
  92.1 42.8 %all-gather.2.cloned.1.call-done = bf16[256,6144]{1,0:T(8,128)(2,1)} async-done(((bf16[16,6144]{1,0:T(8,128)(2,1)}), bf16[256,6144]{1,0:T(8,128)(2,1)}) %all-gather.2.cloned.1.call-update) | async-done | bytes 3145744 | tf_op jit(solution)/shard_map/all_gather | solution.py:121
  134.9 4.2 %convolution_divide_fusion = f32[16,256]{1,0:T(8,128)} fusion(bf16[16,6144]{1,0:T(8,128)(2,1)} %multiply_convert_fusion, bf16[256,6144]{1,0:T(8,128)(2,1)} %all-gather.2.cloned.1.call-done, f32[]{:T(128)} %reduce_sum.38), kind=kOutput, calls=%fused_computation.1 | convolution fusion | flops 50335744 | bytes 3358724 | tf_op jit(solution)/shard_map/dot_general | solution.py:96
  (25 shorter events, 0.9 us)
Async XLA Ops:
  6.5 13.1 %copy-start = (f32[16,6144]{1,0:T(8,128)S(1)}, f32[16,6144]{1,0:T(8,128)}, u32[]{:S(2)}) copy-start(f32[16,6144]{1,0:T(8,128)} %param.4) | copy-start | bytes 1179652
  6.5 128.4 %all-gather.2.cloned.1.call-start = ((), (), s32[]{:S(2)}) async-start(), calls=%async_computation | async-start | bytes 3342336 | tf_op jit(solution)/shard_map/all_gather | solution.py:121
  7.6 11.9 %collective-permute-start = (f32[3,6144]{1,0:T(4,128)S(1)}, f32[3,6144]{1,0:T(4,128)S(1)}, u32[]{:S(2)}, u32[]{:S(2)}) collective-permute-start(f32[3,6144]{1,0:T(4,128)S(1)} %get-tuple-element.10), channel_id=1, source_target_pairs={{0,1},{1,2},{2,3},{3,4},{4,5},{5,6},{6,7},{7,8},{8,9},{9,10},{10,1... | collective-permute-start | bytes 221192 | tf_op jit(solution)/shard_map/ppermute | solution.py:17
  10.1 9.5 %collective-permute-start.1 = (f32[3,6144]{1,0:T(4,128)S(1)}, f32[3,6144]{1,0:T(4,128)S(1)}, u32[]{:S(2)}, u32[]{:S(2)}) collective-permute-start(f32[3,6144]{1,0:T(4,128)S(1)} %get-tuple-element.11), channel_id=1, source_target_pairs={{1,0},{2,1},{3,2},{4,3},{5,4},{6,5},{7,6},{8,7},{9,8},{10,9},{11,1... | collective-permute-start | bytes 221192 | tf_op jit(solution)/shard_map/ppermute | solution.py:19
Sparse Core Ops, SparseCore 0:
  92.2 42.6 all-gather.1
where the time goes:
time: 146 us
  blocking collectives  63.8 us (44%)
  waiting for transfers between devices  42.9 us (29%)
  between operations  14.3 us (10%)
  local copies, waits for them, and re-layouts  10 us (7%)
  other arithmetic  7.05 us (5%)
  matrix products  4.17 us (3%)
  starting transfers between devices  3.7 us (3%)
    psum x1, blocking collectives, shards(): expected = lax.psum(local_total, 'blk') / denominator  63.8 us
    all_gather x1, waiting for transfers between devices, shards(): lax.all_gather(zscores, 'blk', axis=0, tiled=True)  42.8 us
    dot_general x1, matrix products, cross_block(): lax.dot_general(left, right, (((1,), (1,)), ((), ())), preferred_element_...  4.17 us
    scatter x1, local copies, waits for them, and re-layouts, shards(): kept_bins = jnp.ones((col_count,), jnp.float32).at[masked_bins].set(0.0)  2.95 us
  transfers between devices with their start and end apart: 3, of which 1 were waited for; matrix products, arithmetic and copies ran while one was open for 5% of the time, Pallas kernels for 0%

commit v1 on v0

--- a/solution.py
+++ b/solution.py
@@ -1,9 +1,26 @@
+import functools
 import jax
 import jax.numpy as jnp
 from jax import lax
 from jax.sharding import PartitionSpec as P
 
 WMAX = 3
+
+
+def produce_sections_all(sheet, a_name):
+    piece_next, outer, s_next = (lax.psum(1, a_name), lax.axis_index(a_name), sheet.shape[0])
+    raw_out, out_arr = (sheet, 1)
+    while out_arr < piece_next:
+        windows = []
+        for m in range(piece_next):
+            windows.append((m, (m - out_arr) % piece_next))
+        raw_out = jnp.concatenate([raw_out, lax.ppermute(raw_out, a_name, windows)], axis=0)
+        out_arr = 2 * out_arr
+    t1 = jnp.roll(raw_out, outer * s_next, axis=0)
+    return t1
+
+
+resolve_the_loads = functools.partial(produce_sections_all, a_name="blk")
 
 
 def with_halo(cells, sides, width):
@@ -118,7 +135,7 @@
     kept_bins = jnp.ones((col_count,), jnp.float32).at[masked_bins].set(0.0)
     kept_rows = lax.dynamic_slice_in_dim(kept_bins, first_bin + first_row, rows_here)
     zscores, kept_total = normalize(smoothed, expected_map, kept_rows, kept_bins)
-    return cross_block(zscores, lax.all_gather(zscores, "blk", axis=0, tiled=True)) / kept_total
+    return cross_block(zscores, resolve_the_loads(zscores)) / kept_total
 
 
 def solution(mesh):

time: 146 us -> 199 us (1.36)
  waiting for transfers between devices: 42.9 us -> 100 us
  between operations: 14.3 us -> 0.99 us
  local copies, waits for them, and re-layouts: 10 us -> 18.1 us
    ppermute x0 -> x4, waiting for transfers between devices: none -> 100 us  [produce_sections_all(): lax.ppermute(raw_out, a_name, windows)]
    all_gather x1 -> x0, waiting for transfers between devices: 42.8 us -> none  [shards(): lax.all_gather(zscores, 'blk', axis=0, tiled=True)]
    unnamed x8 -> x16, local copies, waits for them, and re-layouts: 0.47 us -> 7.23 us
  transfers between devices with their start and end apart: 3 -> 6, of which waited for: 1 -> 4; matrix products, arithmetic and copies ran while one was open for 5% -> 5% of each run, Pallas kernels for 0% -> 0%
where the time goes in v1:
time: 199 us
  waiting for transfers between devices  100 us (50%)
  blocking collectives  63.8 us (32%)
  local copies, waits for them, and re-layouts  18.1 us (9%)
  other arithmetic  8.05 us (4%)
  matrix products  4 us (2%)
  starting transfers between devices  3.88 us (2%)
    ppermute x4, waiting for transfers between devices, produce_sections_all(): lax.ppermute(raw_out, a_name, windows)  100 us
    psum x1, blocking collectives, shards(): expected = lax.psum(local_total, 'blk') / denominator  63.8 us
    unnamed x16, local copies, waits for them, and re-layouts  7.23 us
    dot_general x1, matrix products, cross_block(): lax.dot_general(left, right, (((1,), (1,)), ((), ())), preferred_element_...  4 us
  transfers between devices with their start and end apart: 6, of which 4 were waited for; matrix products, arithmetic and copies ran while one was open for 5% of the time, Pallas kernels for 0%

profile of v1, /device:TPU:0, one launch (start us, length us, event | category | flops | bytes accessed | tf_op | source)
XLA Modules:
  0.0 198.8 jit_solution(1254043987764885319)
XLA Ops:
  0.0 1.1 fusion.20
  1.1 2.4 %collective-permute-start = (f32[3,6144]{1,0:T(4,128)S(1)}, f32[3,6144]{1,0:T(4,128)S(1)}, u32[]{:S(2)}, u32[]{:S(2)}) collective-permute-start(f32[3,6144]{1,0:T(4,128)S(1)} %get-tuple-element.12), channel_id=1, source_target_pairs={{0,1},{1,2},{2,3},{3,4},{4,5},{5,6},{6,7},{7,8},{8,9},{9,10},{10,1... | collective-permute-start | bytes 221192 | tf_op jit(solution)/shard_map/ppermute | solution.py:34
  3.5 1.3 collective-permute-start.1
  5.5 0.7 compare_select_fusion
  6.2 2.9 %scatter_custom_fusion = f32[6144]{0:T(1024)S(1)} fusion(s32[384]{0:T(512)S(1)} %compare_select_fusion, f32[384]{0:T(512)S(1)} %broadcast.31, f32[]{:T(128)} %constant.70.clone.1), kind=kCustom, calls=%fused_computation.62 | custom fusion | bytes 24580 | tf_op jit(solution)/shard_map/scatter | solution.py:135
  9.1 0.6 reduce_sum.38
  9.8 0.8 slice.102
  10.8 0.8 fusion.16
  12.2 0.8 rev.19
  13.0 1.3 select_maximum_fusion
  14.6 1.5 fusion.8
  16.1 0.8 rev.20
  17.6 0.5 dynamic_update_slice.3
  18.3 63.8 %psum.7 = f32[6144]{0:T(1024)S(1)} all-reduce(f32[6144]{0:T(1024)S(1)} %slice_add_fusion.18), channel_id=1, replica_groups=mesh['groups'=2,'blk'=16] {'blk'}, use_global_device_ids=true, to_apply=%region_1.2 | all-reduce | flops 6144 | bytes 49152 | tf_op jit(solution)/shard_map/psum | solution.py:133
  83.1 0.8 rev.23
  84.1 0.6 broadcast_divide_fusion
  84.9 0.6 add_rsqrt_fusion
  85.5 0.8 constant_dynamic-update-slice_fusion.9
  86.3 3.2 %collective-permute-done.2 = bf16[16,6144]{1,0:T(8,128)(2,1)S(1)} collective-permute-done((bf16[16,6144]{1,0:T(8,128)(2,1)S(1)}, bf16[16,6144]{1,0:T(8,128)(2,1)S(1)}, u32[]{:S(2)}, u32[]{:S(2)}) %collective-permute-start.2) | collective-permute-done | bytes 196640 | tf_op jit(solution)/shard_map/ppermute | solution.py:17
  89.6 9.4 %collective-permute-done.3 = bf16[32,6144]{1,0:T(8,128)(2,1)S(1)} collective-permute-done((bf16[32,6144]{1,0:T(8,128)(2,1)S(1)}, bf16[32,6144]{1,0:T(8,128)(2,1)S(1)}, u32[]{:S(2)}, u32[]{:S(2)}) %collective-permute-start.3) | collective-permute-done | bytes 393248 | tf_op jit(solution)/shard_map/ppermute | solution.py:17
  99.1 19.6 %collective-permute-done.4 = bf16[64,6144]{1,0:T(8,128)(2,1)S(1)} collective-permute-done((bf16[64,6144]{1,0:T(8,128)(2,1)S(1)}, bf16[64,6144]{1,0:T(8,128)(2,1)S(1)}, u32[]{:S(2)}, u32[]{:S(2)}) %collective-permute-start.4) | collective-permute-done | bytes 786464 | tf_op jit(solution)/shard_map/ppermute | solution.py:17
  119.0 0.7 constant_dynamic-update-slice_fusion.8
  119.7 0.8 constant_dynamic-update-slice_fusion.7
  120.4 1.0 constant_dynamic-update-slice_fusion.6
  121.4 67.8 %collective-permute-done.5 = bf16[128,6144]{1,0:T(8,128)(2,1)S(1)} collective-permute-done((bf16[128,6144]{1,0:T(8,128)(2,1)S(1)}, bf16[128,6144]{1,0:T(8,128)(2,1)S(1)}, u32[]{:S(2)}, u32[]{:S(2)}) %collective-permute-start.5) | collective-permute-done | bytes 1572896 | tf_op jit(solution)/shard_map/ppermute | solution.py:17
  189.2 1.3 constant_dynamic-update-slice_fusion.5
  190.5 0.7 constant_dynamic-update-slice_fusion.4
  191.2 0.7 constant_dynamic-update-slice_fusion.3
  191.9 0.8 constant_dynamic-update-slice_fusion.2
  192.6 0.9 constant_dynamic-update-slice_fusion.1
  193.6 1.3 constant_dynamic-update-slice_fusion
  194.8 4.0 %fusion.2 = f32[16,256]{1,0:T(8,128)} fusion(bf16[16,6144]{1,0:T(8,128)(2,1)S(1)} %get-tuple-element.6, bf16[512,6144]{1,0:T(8,128)(2,1)} %constant_dynamic-update-slice_fusion, s32[]{:T(128)S(6)} %select_n.50, f32[]{:T(128)} %reduce_sum.38), kind=kOutput, calls=%fused_computation.4 | convolution fusion | flops 50335744 | bytes 3359236 | tf_op jit(solution)/shard_map/dot_general | solution.py:113
  (42 shorter events, 3.7 us)
Async XLA Ops:
  0.0 14.6 %copy-start = (f32[16,6144]{1,0:T(8,128)S(1)}, f32[16,6144]{1,0:T(8,128)}, u32[]{:S(2)}) copy-start(f32[16,6144]{1,0:T(8,128)} %param.4) | copy-start | bytes 1179652
  1.1 11.9 %collective-permute-start = (f32[3,6144]{1,0:T(4,128)S(1)}, f32[3,6144]{1,0:T(4,128)S(1)}, u32[]{:S(2)}, u32[]{:S(2)}) collective-permute-start(f32[3,6144]{1,0:T(4,128)S(1)} %get-tuple-element.12), channel_id=1, source_target_pairs={{0,1},{1,2},{2,3},{3,4},{4,5},{5,6},{6,7},{7,8},{8,9},{9,10},{10,1... | collective-permute-start | bytes 221192 | tf_op jit(solution)/shard_map/ppermute | solution.py:34
  3.5 9.5 %collective-permute-start.1 = (f32[3,6144]{1,0:T(4,128)S(1)}, f32[3,6144]{1,0:T(4,128)S(1)}, u32[]{:S(2)}, u32[]{:S(2)}) collective-permute-start(f32[3,6144]{1,0:T(4,128)S(1)} %get-tuple-element.13), channel_id=1, source_target_pairs={{1,0},{2,1},{3,2},{4,3},{5,4},{6,5},{7,6},{8,7},{9,8},{10,9},{11,1... | collective-permute-start | bytes 221192 | tf_op jit(solution)/shard_map/ppermute | solution.py:36
  86.3 3.2 %collective-permute-start.2 = (bf16[16,6144]{1,0:T(8,128)(2,1)S(1)}, bf16[16,6144]{1,0:T(8,128)(2,1)S(1)}, u32[]{:S(2)}, u32[]{:S(2)}) collective-permute-start(bf16[16,6144]{1,0:T(8,128)(2,1)S(1)} %get-tuple-element.6), channel_id=1, source_target_pairs={{0,15},{1,0},{2,1},{3,2},{4,3},{5,4},{6,5},{7,6},{8,7},{9,8},{10,9... | collective-permute-start | bytes 589832 | tf_op jit(solution)/shard_map/ppermute | solution.py:17
  89.5 9.5 %collective-permute-start.3 = (bf16[32,6144]{1,0:T(8,128)(2,1)S(1)}, bf16[32,6144]{1,0:T(8,128)(2,1)S(1)}, u32[]{:S(2)}, u32[]{:S(2)}) collective-permute-start(bf16[32,6144]{1,0:T(8,128)(2,1)S(1)} %pad_maximum_fusion.2), channel_id=1, source_target_pairs={{0,14},{1,15},{2,0},{3,1},{4,2},{5,3},{6,4},{7,5},{8,6},{9,7},{10,... | collective-permute-start | bytes 1179656 | tf_op jit(solution)/shard_map/ppermute | solution.py:17
  99.1 19.7 %collective-permute-start.4 = (bf16[64,6144]{1,0:T(8,128)(2,1)S(1)}, bf16[64,6144]{1,0:T(8,128)(2,1)S(1)}, u32[]{:S(2)}, u32[]{:S(2)}) collective-permute-start(bf16[64,6144]{1,0:T(8,128)(2,1)S(1)} %pad_maximum_fusion.1), channel_id=1, source_target_pairs={{0,12},{1,13},{2,14},{3,15},{4,0},{5,1},{6,2},{7,3},{8,4},{9,5},{1... | collective-permute-start | bytes 2359304 | tf_op jit(solution)/shard_map/ppermute | solution.py:17
  118.9 70.3 %collective-permute-start.5 = (bf16[128,6144]{1,0:T(8,128)(2,1)S(1)}, bf16[128,6144]{1,0:T(8,128)(2,1)S(1)}, u32[]{:S(2)}, u32[]{:S(2)}) collective-permute-start(bf16[128,6144]{1,0:T(8,128)(2,1)S(1)} %pad_maximum_fusion), channel_id=1, source_target_pairs={{0,8},{1,9},{2,10},{3,11},{4,12},{5,13},{6,14},{7,15},{8,0},{9,1},... | collective-permute-start | bytes 4718600 | tf_op jit(solution)/shard_map/ppermute | solution.py:17
